TPU v7x, 32 devices: a whole 2x2x4 slice. The times are simulated.
32 devices in a mesh: groups: 2 (over y), dp: 4 (over z), task: 4 (over x, core).
Axes of the slice: x: 2, y: 2, z: 4, core: 2. Of those that a mesh axis runs over, the one named last changes fastest.
Arguments:
- coords: bfloat16 [3, 6144], P(None, ('groups', 'dp')), parts along dimension 1, may hold values from 0 to 1
- lengthscales: float32 [6], P('groups'), parts along dimension 0, may hold values from 0.15 to 0.5
- vectors: bfloat16 [2, 6144, 256], P(None, ('groups', 'dp'), 'task'), parts along dimension 1, may hold values from -6 to 6
- mixing: bfloat16 [512, 256], P('groups'), parts along dimension 0, may hold values from -0.078125 to 0.078125
- noise: float32 [512], P(('groups', 'task')), parts along dimension 0, may hold values from 0.1 to 1
Outputs:
- product: bfloat16 [2, 6144, 256], P(None, ('groups', 'dp'), 'task'), parts along dimension 1
- gradient: float32 [512, 256], P(('groups', 'task')), parts along dimension 0
There are 2 independent parts, one for each index of `groups`. A program takes and returns all parts, laid end to end along the dimension named above; each array names one. Nothing has to cross between parts.
All inputs are finite; a program needn't handle non-finite values.
Results may differ from a plain program's by a relative error of at most 0.0056.
Values may be sent and summed in bfloat16 or wider, within the bound.
No kernel may reach another device: no remote copies, remote signals or barrier semaphores. Data moves between devices by JAX's collectives and lax.ppermute only.
A program may use at most 64 MiB of HBM per device.

v0:
```python
import jax
import jax.numpy as jnp
from jax import lax
from jax.sharding import PartitionSpec as P


def kernel_tile(left, right):
    diff = left[:, :, None] - right[:, None, :]
    return jnp.exp(0.1 - jnp.sqrt(jnp.sum(diff * diff, axis=0) + 0.01))


def shift(x, axis, k, n):
    return lax.ppermute(x, axis, [(i, (i + k) % n) for i in range(n)])


def sum_over(x, axis, n):
    if n == 4:
        got = [shift(x, axis, k, n) for k in range(1, n)]
        even = lax.axis_index(axis) % 2 == 0
        first = x + jnp.where(even, got[2], got[0])
        second = got[1] + jnp.where(even, got[0], got[2])
        return first + second
    if n & n - 1:
        return lax.psum(x, axis)
    step = 1
    while step < n:
        x = x + lax.ppermute(x, axis, [(i, i ^ step) for i in range(n)])
        step *= 2
    return x


def per_device(coords, lengthscales, vectors, mixing, noise):
    n_rows = coords.shape[1]
    local_tasks = vectors.shape[2]
    n_dp = lax.axis_size("dp")
    task_start = lax.axis_index("task") * local_tasks
    inverse = 1.0 / lengthscales
    own_scaled = coords.astype(jnp.float32) * inverse[:, None]

    def block(right_coords, values):
        right = right_coords.astype(jnp.float32) * inverse[:, None]
        tile = kernel_tile(own_scaled, right).astype(jnp.bfloat16)
        return jnp.einsum("nr,srm->snm", tile, values, preferred_element_type=jnp.float32)

    task_input = vectors
    if n_dp <= 4:
        moved = [shift(vectors, "dp", k, n_dp) for k in range(1, n_dp)]
        if n_dp == 4:
            first = shift(coords, "dp", 1, n_dp)
            peer_coords = [first, shift(first, "dp", 1, n_dp), shift(coords, "dp", 3, n_dp)]
        else:
            peer_coords = [shift(coords, "dp", k, n_dp) for k in range(1, n_dp)]
        task_input = lax.optimization_barrier((vectors, peer_coords))[0]
        summed = block(coords, vectors)
        order = [1, 3, 2] if n_dp == 4 else list(range(1, n_dp))
        for k in order:
            summed = summed + block(peer_coords[k - 1], moved[k - 1])
    else:

        def ring(_, carry):
            accum, right_coords, values = carry
            right_coords = shift(right_coords, "dp", 1, n_dp)
            values = shift(values, "dp", 1, n_dp)
            return (accum + block(right_coords, values), right_coords, values)

        summed = block(coords, vectors)
        summed = lax.fori_loop(0, n_dp - 1, ring, (summed, coords, vectors))[0]
    n_task = lax.axis_size("task")
    copies = jnp.broadcast_to(task_input[None], (n_task,) + vectors.shape)
    task_blocks = lax.all_to_all(copies, "task", 0, 0, tiled=True)
    images = summed.astype(jnp.bfloat16)
    signs = jnp.array([1.0, -1.0], jnp.bfloat16)
    signed = images * signs[:, None, None]
    partial_grad = jnp.einsum(
        "sna,ksnb->akb", signed, task_blocks, preferred_element_type=jnp.float32
    ).reshape(local_tasks, n_task * local_tasks)
    total = sum_over(partial_grad, "dp", n_dp)
    gather_input = lax.optimization_barrier((images, task_blocks))[0]
    whole_images = lax.all_gather(
        jnp.transpose(gather_input, (2, 0, 1)), "task", axis=0, tiled=True
    )
    own_rows = lax.dynamic_slice_in_dim(mixing, task_start, local_tasks, 0)
    mixed = jnp.einsum("asn,ca->snc", whole_images, own_rows, preferred_element_type=jnp.float32)
    product = (mixed + noise[None, None, :] * vectors.astype(jnp.float32)).astype(jnp.bfloat16)
    gradient = total / (2.0 * n_rows * n_dp)
    return (product, gradient)


def solution(mesh):
    in_specs = (
        P(None, ("groups", "dp")),
        P("groups"),
        P(None, ("groups", "dp"), "task"),
        P("groups", None),
        P(("groups", "task")),
    )
    out_specs = (P(None, ("groups", "dp"), "task"), P(("groups", "task"), None))
    return jax.shard_map(
        per_device, mesh=mesh, in_specs=in_specs, out_specs=out_specs, check_vma=False
    )
```

profile of v0, /device:TPU:0, one launch (start us, length us, event | category | flops | bytes accessed | tf_op | source)
XLA Modules:
  0.0 54.8 jit_solution(17863950669732573691)
XLA Ops:
  0.7 3.1 %collective-permute-start = (bf16[3,768]{1,0:T(4,128)(2,1)}, bf16[3,768]{1,0:T(4,128)(2,1)S(1)}, u32[]{:S(2)}, u32[]{:S(2)}) collective-permute-start(bf16[3,768]{1,0:T(4,128)(2,1)} %param.6), channel_id=1, source_target_pairs={{0,4},{4,8},{8,12},{12,0},{1,5},{5,9},{9,13},{13,1},{2,6},{6,10},{... | collective-permute-start | bytes 13832 | tf_op jit(solution)/shard_map/ppermute | solution.py:13
  3.7 2.1 %collective-permute-start.2 = (bf16[3,768]{1,0:T(4,128)(2,1)}, bf16[3,768]{1,0:T(4,128)(2,1)S(1)}, u32[]{:S(2)}, u32[]{:S(2)}) collective-permute-start(bf16[3,768]{1,0:T(4,128)(2,1)} %param.6), channel_id=1, source_target_pairs={{0,12},{4,0},{8,4},{12,8},{1,13},{5,1},{9,5},{13,9},{2,14},{6,2},{... | collective-permute-start | bytes 13832 | tf_op jit(solution)/shard_map/ppermute | solution.py:13
  5.8 3.8 %collective-permute-start.3 = (bf16[2,768,64]{1,2,0:T(8,128)(2,1)}, bf16[2,768,64]{1,2,0:T(8,128)(2,1)S(1)}, u32[]{:S(2)}, u32[]{:S(2)}) collective-permute-start(bf16[2,768,64]{1,2,0:T(8,128)(2,1)} %param.8), channel_id=1, source_target_pairs={{0,12},{4,0},{8,4},{12,8},{1,13},{5,1},{9,5},{13,9},{2,14},{6,2},{... | collective-permute-start | bytes 589832 | tf_op jit(solution)/shard_map/ppermute | solution.py:13
  9.7 0.7 %collective-permute-start.4 = (bf16[3,768]{1,0:T(4,128)(2,1)S(1)}, bf16[3,768]{1,0:T(4,128)(2,1)S(1)}, u32[]{:S(2)}, u32[]{:S(2)}) collective-permute-start(bf16[3,768]{1,0:T(4,128)(2,1)S(1)} %collective-permute-done), channel_id=1, source_target_pairs={{0,4},{4,8},{8,12},{12,0},{1,5},{5,9},{9,13},{13,1},{2,6},{6,10},{... | collective-permute-start | bytes 13832 | tf_op jit(solution)/shard_map/ppermute | solution.py:13
  10.4 0.7 %broadcast_divide_fusion = f32[3]{0:T(128)S(1)} fusion(f32[3]{0:T(128)} %param.7), kind=kLoop, calls=%fused_computation.28 | loop fusion | flops 3 | bytes 24 | tf_op jit(solution)/shard_map/div | solution.py:37
  11.0 11.9 %collective-permute-done.4 = bf16[3,768]{1,0:T(4,128)(2,1)S(1)} collective-permute-done((bf16[3,768]{1,0:T(4,128)(2,1)S(1)}, bf16[3,768]{1,0:T(4,128)(2,1)S(1)}, u32[]{:S(2)}, u32[]{:S(2)}) %collective-permute-start.4) | collective-permute-done | bytes 4640 | tf_op jit(solution)/shard_map/ppermute | solution.py:13
  22.9 1.9 %broadcast_in_dim.2 = bf16[4,2,768,64]{2,3,1,0:T(8,128)(2,1)} broadcast(bf16[2,768,64]{1,2,0:T(8,128)(2,1)} %param.8), dimensions={1,2,3} | broadcast | bytes 983040 | tf_op jit(solution)/shard_map/broadcast_in_dim | solution.py:69
  24.8 3.5 %all-to-all-start = ((bf16[4,2,768,64]{2,3,1,0:T(8,128)(2,1)}), bf16[4,2,768,64]{2,3,1,0:T(8,128)(2,1)S(1)}, u32[]{:S(2)}, u32[]{:S(2)}) async-start(bf16[4,2,768,64]{2,3,1,0:T(8,128)(2,1)} %broadcast_in_dim.2), calls=%async_computation | async-start | bytes 1572864 | tf_op jit(solution)/shard_map/all_to_all | solution.py:70
  28.3 0.1 convert_multiply_fusion
  28.4 4.7 %multiply_reduce_fusion.2 = (f32[768,768]{1,0:T(8,128)S(1)}, f32[768,768]{1,0:T(8,128)S(1)}, f32[768,768]{1,0:T(8,128)S(1)}, f32[768,768]{1,0:T(8,128)S(1)}) fusion(f32[3,768]{1,0:T(4,128)S(1)} %get-tuple-element.11, f32[3,768]{1,0:T(4,128)S(1)} %get-tuple-element.13, f32[3,768]{1,0:T(4,128)S(1)} %get-tuple-element.12, f32[3,768]{1,0:T(4,128)S(1)} %get-tuple-element.10), kind=kLoop, calls=%fused_computation.2 | loop fusion | flops 18874368 | bytes 9474048 | tf_op jit(solution)/shard_map/reduce_sum | solution.py:9
  33.0 1.1 %fusion = f32[768,128]{0,1:S(1)} fusion(bf16[768,128]{0,1:T(8,128)(2,1)S(1)} %bitcast.35, f32[768,768]{1,0:T(8,128)S(1)} %get-tuple-element.9), kind=kOutput, calls=%fused_computation.9 | convolution fusion | flops 152764416 | bytes 2949120
  34.1 1.1 %fusion.1 = f32[768,128]{0,1:S(1)} fusion(bf16[768,128]{0,1:T(8,128)(2,1)S(1)} %bitcast.42, f32[768,768]{1,0:T(8,128)S(1)} %get-tuple-element.6), kind=kOutput, calls=%fused_computation.10 | convolution fusion | flops 152764416 | bytes 2949120
  35.2 1.1 %fusion.2 = f32[768,128]{0,1:S(1)} fusion(bf16[768,128]{0,1:T(8,128)(2,1)S(1)} %bitcast.41, f32[768,768]{1,0:T(8,128)S(1)} %get-tuple-element.7), kind=kOutput, calls=%fused_computation.11 | convolution fusion | flops 152764416 | bytes 2949120
  36.4 1.1 %fusion.3 = f32[768,128]{0,1:S(1)} fusion(bf16[768,128]{0,1:T(8,128)(2,1)S(1)} %bitcast.40, f32[768,768]{1,0:T(8,128)S(1)} %get-tuple-element.8), kind=kOutput, calls=%fused_computation.12 | convolution fusion | flops 152764416 | bytes 2949120
  37.5 0.1 fusion.5
  37.6 2.3 %all-to-all-done = bf16[4,2,768,64]{2,3,1,0:T(8,128)(2,1)S(1)} async-done(((bf16[4,2,768,64]{2,3,1,0:T(8,128)(2,1)}), bf16[4,2,768,64]{2,3,1,0:T(8,128)(2,1)S(1)}, u32[]{:S(2)}, u32[]{:S(2)}) %all-to-all-start) | async-done | bytes 786464 | tf_op jit(solution)/shard_map/all_to_all | solution.py:70
  39.9 0.5 convolution_bitcast_fusion
  40.4 0.1 copy.9
  40.5 0.1 reshape.16
  40.7 2.0 %collective-permute-start.7 = (f32[64,256]{1,0:T(8,128)S(1)}, f32[64,256]{1,0:T(8,128)S(1)}, u32[]{:S(2)}, u32[]{:S(2)}) collective-permute-start(f32[64,256]{1,0:T(8,128)S(1)} %reshape.16), channel_id=1, source_target_pairs={{0,4},{4,8},{8,12},{12,0},{1,5},{5,9},{9,13},{13,1},{2,6},{6,10},{... | collective-permute-start | bytes 196616 | tf_op jit(solution)/shard_map/ppermute | solution.py:13
  42.7 3.1 %collective-permute-start.8 = (f32[64,256]{1,0:T(8,128)S(1)}, f32[64,256]{1,0:T(8,128)S(1)}, u32[]{:S(2)}, u32[]{:S(2)}) collective-permute-start(f32[64,256]{1,0:T(8,128)S(1)} %reshape.16), channel_id=1, source_target_pairs={{0,8},{4,12},{8,0},{12,4},{1,9},{5,13},{9,1},{13,5},{2,10},{6,14},... | collective-permute-start | bytes 196616 | tf_op jit(solution)/shard_map/ppermute | solution.py:13
  45.8 7.4 %all_gather.3 = bf16[256,2,768]{2,0,1:T(8,128)(2,1)S(1)} all-gather(bf16[64,2,768]{2,0,1:T(8,128)(2,1)S(1)} %bitcast.34), channel_id=1, replica_groups=mesh['groups'=2,'dp'=4,'task'=4] {'task'}, dimensions={0}, use_global_device_ids=true | all-gather | bytes 983040 | tf_op jit(solution)/shard_map/all_gather | solution.py:79
  53.2 0.9 %fusion.4 = bf16[2,768,64]{1,2,0:T(8,128)(2,1)} fusion(bf16[256,2,768]{2,0,1:T(8,128)(2,1)S(1)} %all_gather.3, bf16[2,768,64]{1,2,0:T(8,128)(2,1)S(1)} %copy-done.1, f32[64]{0:T(128)S(1)} %copy-done.3, bf16[256,256]{1,0:T(8,128)(2,1)S(1)} %copy-done, s32[]{:T(128)S(6)} %select_n.22), kind=kOutput, calls=%fused_computation.13 | convolution fusion | flops 50724864 | bytes 1212932 | tf_op jit(solution)/shard_map/asn,ca->snc/dot_general | solution.py:83
  54.2 0.7 %add_multiply_fusion = f32[64,256]{1,0:T(8,128)} fusion(f32[64,256]{1,0:T(8,128)S(1)} %collective-permute-done.8, f32[64,256]{1,0:T(8,128)S(1)} %collective-permute-done.7, f32[64,256]{1,0:T(8,128)S(1)} %collective-permute-done.6, f32[64,256]{1,0:T(8,128)S(1)} %reshape.16, pred[]{:T(512)S(6)} %eq.5), kind=kLoop, calls=%fused_computation.20 | loop fusion | flops 98304 | bytes 327681 | tf_op jit(solution)/shard_map/div | solution.py:85
  (21 shorter events, 0.1 us)
Async XLA Ops:
  0.6 52.6 %copy-start = (bf16[256,256]{1,0:T(8,128)(2,1)S(1)}, bf16[256,256]{1,0:T(8,128)(2,1)}, u32[]{:S(2)}) copy-start(bf16[256,256]{1,0:T(8,128)(2,1)} %param.9) | copy-start | bytes 393220
  0.6 27.6 %copy-start.2 = (bf16[3,768]{1,0:T(4,128)(2,1)S(1)}, bf16[3,768]{1,0:T(4,128)(2,1)}, u32[]{:S(2)}) copy-start(bf16[3,768]{1,0:T(4,128)(2,1)} %param.6) | copy-start | bytes 13828
  0.7 9.0 %collective-permute-start = (bf16[3,768]{1,0:T(4,128)(2,1)}, bf16[3,768]{1,0:T(4,128)(2,1)S(1)}, u32[]{:S(2)}, u32[]{:S(2)}) collective-permute-start(bf16[3,768]{1,0:T(4,128)(2,1)} %param.6), channel_id=1, source_target_pairs={{0,4},{4,8},{8,12},{12,0},{1,5},{5,9},{9,13},{13,1},{2,6},{6,10},{... | collective-permute-start | bytes 13832 | tf_op jit(solution)/shard_map/ppermute | solution.py:13
  3.7 7.3 %collective-permute-start.2 = (bf16[3,768]{1,0:T(4,128)(2,1)}, bf16[3,768]{1,0:T(4,128)(2,1)S(1)}, u32[]{:S(2)}, u32[]{:S(2)}) collective-permute-start(bf16[3,768]{1,0:T(4,128)(2,1)} %param.6), channel_id=1, source_target_pairs={{0,12},{4,0},{8,4},{12,8},{1,13},{5,1},{9,5},{13,9},{2,14},{6,2},{... | collective-permute-start | bytes 13832 | tf_op jit(solution)/shard_map/ppermute | solution.py:13
  5.8 28.3 %collective-permute-start.1 = (bf16[2,768,64]{1,2,0:T(8,128)(2,1)}, bf16[2,768,64]{1,2,0:T(8,128)(2,1)S(1)}, u32[]{:S(2)}, u32[]{:S(2)}) collective-permute-start(bf16[2,768,64]{1,2,0:T(8,128)(2,1)} %param.8), channel_id=1, source_target_pairs={{0,4},{4,8},{8,12},{12,0},{1,5},{5,9},{9,13},{13,1},{2,6},{6,10},{... | collective-permute-start | bytes 589832 | tf_op jit(solution)/shard_map/ppermute | solution.py:13
  5.8 29.4 %collective-permute-start.3 = (bf16[2,768,64]{1,2,0:T(8,128)(2,1)}, bf16[2,768,64]{1,2,0:T(8,128)(2,1)S(1)}, u32[]{:S(2)}, u32[]{:S(2)}) collective-permute-start(bf16[2,768,64]{1,2,0:T(8,128)(2,1)} %param.8), channel_id=1, source_target_pairs={{0,12},{4,0},{8,4},{12,8},{1,13},{5,1},{9,5},{13,9},{2,14},{6,2},{... | collective-permute-start | bytes 589832 | tf_op jit(solution)/shard_map/ppermute | solution.py:13
  9.6 26.7 %collective-permute-start.5 = (bf16[2,768,64]{1,2,0:T(8,128)(2,1)}, bf16[2,768,64]{1,2,0:T(8,128)(2,1)S(1)}, u32[]{:S(2)}, u32[]{:S(2)}) collective-permute-start(bf16[2,768,64]{1,2,0:T(8,128)(2,1)} %param.8), channel_id=1, source_target_pairs={{0,8},{4,12},{8,0},{12,4},{1,9},{5,13},{9,1},{13,5},{2,10},{6,14},... | collective-permute-start | bytes 589832 | tf_op jit(solution)/shard_map/ppermute | solution.py:13
  9.7 13.2 %collective-permute-start.4 = (bf16[3,768]{1,0:T(4,128)(2,1)S(1)}, bf16[3,768]{1,0:T(4,128)(2,1)S(1)}, u32[]{:S(2)}, u32[]{:S(2)}) collective-permute-start(bf16[3,768]{1,0:T(4,128)(2,1)S(1)} %collective-permute-done), channel_id=1, source_target_pairs={{0,4},{4,8},{8,12},{12,0},{1,5},{5,9},{9,13},{13,1},{2,6},{6,10},{... | collective-permute-start | bytes 13832 | tf_op jit(solution)/shard_map/ppermute | solution.py:13
  24.8 15.1 %all-to-all-start = ((bf16[4,2,768,64]{2,3,1,0:T(8,128)(2,1)}), bf16[4,2,768,64]{2,3,1,0:T(8,128)(2,1)S(1)}, u32[]{:S(2)}, u32[]{:S(2)}) async-start(bf16[4,2,768,64]{2,3,1,0:T(8,128)(2,1)} %broadcast_in_dim.2), calls=%async_computation | async-start | bytes 1572864 | tf_op jit(solution)/shard_map/all_to_all | solution.py:70
  28.4 4.7 %copy-start.1 = (bf16[2,768,64]{1,2,0:T(8,128)(2,1)S(1)}, bf16[2,768,64]{1,2,0:T(8,128)(2,1)}, u32[]{:S(2)}) copy-start(bf16[2,768,64]{1,2,0:T(8,128)(2,1)} %param.8) | copy-start | bytes 589828
  36.4 3.5 %copy-start.4 = (bf16[2]{0:T(256)(128)(2,1)S(1)}, bf16[2]{0:T(256)(128)(2,1)}, u32[]{:S(2)}) copy-start(bf16[2]{0:T(256)(128)(2,1)} %constant.38.clone) | copy-start | bytes 16
  37.5 15.8 %copy-start.3 = (f32[64]{0:T(128)S(1)}, f32[64]{0:T(128)}, u32[]{:S(2)}) copy-start(f32[64]{0:T(128)} %param.10) | copy-start | bytes 772
  40.6 13.5 %collective-permute-start.6 = (f32[64,256]{1,0:T(8,128)S(1)}, f32[64,256]{1,0:T(8,128)S(1)}, u32[]{:S(2)}, u32[]{:S(2)}) collective-permute-start(f32[64,256]{1,0:T(8,128)S(1)} %reshape.16), channel_id=1, source_target_pairs={{0,12},{4,0},{8,4},{12,8},{1,13},{5,1},{9,5},{13,9},{2,14},{6,2},{... | collective-permute-start | bytes 196616 | tf_op jit(solution)/shard_map/ppermute | solution.py:13
  40.7 13.5 %collective-permute-start.7 = (f32[64,256]{1,0:T(8,128)S(1)}, f32[64,256]{1,0:T(8,128)S(1)}, u32[]{:S(2)}, u32[]{:S(2)}) collective-permute-start(f32[64,256]{1,0:T(8,128)S(1)} %reshape.16), channel_id=1, source_target_pairs={{0,4},{4,8},{8,12},{12,0},{1,5},{5,9},{9,13},{13,1},{2,6},{6,10},{... | collective-permute-start | bytes 196616 | tf_op jit(solution)/shard_map/ppermute | solution.py:13
  42.7 11.5 %collective-permute-start.8 = (f32[64,256]{1,0:T(8,128)S(1)}, f32[64,256]{1,0:T(8,128)S(1)}, u32[]{:S(2)}, u32[]{:S(2)}) collective-permute-start(f32[64,256]{1,0:T(8,128)S(1)} %reshape.16), channel_id=1, source_target_pairs={{0,8},{4,12},{8,0},{12,4},{1,9},{5,13},{9,1},{13,5},{2,10},{6,14},... | collective-permute-start | bytes 196616 | tf_op jit(solution)/shard_map/ppermute | solution.py:13
where the time goes:
time: 55.1 us; the launch traced here: 54.8 us
  starting transfers between devices  18.3 us (33%)
  waiting for transfers between devices  14.2 us (26%)
  blocking collectives  7.45 us (14%)
  other arithmetic  6.12 us (11%)
  matrix products  5.86 us (11%)
  local copies, waits for them, and re-layouts  2.13 us (4%)
  between operations  0.74 us (1%)
    ppermute x9, starting transfers between devices, shift(): return lax.ppermute(x, axis, [(i, (i + k) % n) for i in range(n)])  14.8 us
    ppermute x9, waiting for transfers between devices, shift(): return lax.ppermute(x, axis, [(i, (i + k) % n) for i in range(n)])  11.9 us
    all_gather x1, blocking collectives, per_device(): lax.all_gather(jnp.transpose(gather_input, (2, 0, 1)), 'task', axis=0, ti...  7.45 us
    reduce_sum x1, other arithmetic, kernel_tile(): return jnp.exp(0.1 - jnp.sqrt(jnp.sum(diff * diff, axis=0) + 0.01))  4.65 us
    unnamed x4, matrix products  4.41 us
    all_to_all x1, starting transfers between devices, per_device(): task_blocks = lax.all_to_all(copies, 'task', 0, 0, tiled=True)  3.49 us
    all_to_all x1, waiting for transfers between devices, per_device(): task_blocks = lax.all_to_all(copies, 'task', 0, 0, tiled=True)  2.32 us
    broadcast_in_dim x1, local copies, waits for them, and re-layouts, per_device(): copies = jnp.broadcast_to(task_input[None], (n_task,) + vectors.shape)  1.87 us
  transfers between devices with their start and end apart: 10, of which 2 were waited for; matrix products, arithmetic and copies ran while one was open for 23% of the time, Pallas kernels for 0%

commit v1 on v0

--- a/solution.py
+++ b/solution.py
@@ -1,7 +1,36 @@
+import functools
 import jax
 import jax.numpy as jnp
 from jax import lax
 from jax.sharding import PartitionSpec as P
+
+
+def _list_rates(v0, dim_k):
+    r_now = list(v0.shape[1:])
+    r_now[dim_k] *= v0.shape[0]
+    return jnp.moveaxis(v0, 0, dim_k).reshape(r_now)
+
+
+def review_the_sums_all(u, mesh_name):
+    workers = lax.axis_size(mesh_name)
+    state_now = u[None]
+    for rr in range(workers.bit_length() - 1):
+        current_arr = 1 << rr
+        earlier = tuple(((no, no ^ current_arr) for no in range(workers)))
+        aux = lax.ppermute(state_now, axis_name=mesh_name, perm=earlier)
+        item_now = jnp.stack([state_now, aux])
+        prior = lax.axis_index(mesh_name)
+        p_next = prior >> rr & 1
+        state_now = jnp.where(p_next == 0, item_now, item_now[::-1]).reshape(-1, *u.shape)
+    return state_now
+
+
+def mark_domain(body, here_x, join_dim):
+    tmp = review_the_sums_all(body, here_x)
+    return _list_rates(tmp, join_dim)
+
+
+_create_counts = functools.partial(mark_domain, here_x="task", join_dim=0)
 
 
 def kernel_tile(left, right):
@@ -76,9 +105,7 @@
     ).reshape(local_tasks, n_task * local_tasks)
     total = sum_over(partial_grad, "dp", n_dp)
     gather_input = lax.optimization_barrier((images, task_blocks))[0]
-    whole_images = lax.all_gather(
-        jnp.transpose(gather_input, (2, 0, 1)), "task", axis=0, tiled=True
-    )
+    whole_images = _create_counts(jnp.transpose(gather_input, (2, 0, 1)))
     own_rows = lax.dynamic_slice_in_dim(mixing, task_start, local_tasks, 0)
     mixed = jnp.einsum("asn,ca->snc", whole_images, own_rows, preferred_element_type=jnp.float32)
     product = (mixed + noise[None, None, :] * vectors.astype(jnp.float32)).astype(jnp.bfloat16)

time: 55.1 us -> 54.8 us (level)
  blocking collectives: 7.45 us -> 0 us
  waiting for transfers between devices: 14.2 us -> 20.2 us
    all_gather x1 -> x0, blocking collectives: 7.45 us -> none  [per_device(): lax.all_gather(jnp.transpose(gather_input, (2, 0, 1)), 'task', axis=0, ti...]
    ppermute x9, waiting for transfers between devices: 11.9 us -> 16.4 us  [shift(): return lax.ppermute(x, axis, [(i, (i + k) % n) for i in range(n)])]
    ppermute x0 -> x2, waiting for transfers between devices: none -> 1.44 us  [review_the_sums_all(): aux = lax.ppermute(state_now, axis_name=mesh_name, perm=earlier)]
  transfers between devices with their start and end apart: 10 -> 12, of which waited for: 2 -> 6; matrix products, arithmetic and copies ran while one was open for 23% -> 24% of each run, Pallas kernels for 0% -> 0%
where the time goes in v1:
time: 54.8 us; the launch traced here: 54.5 us
  waiting for transfers between devices  20.2 us (37%)
  starting transfers between devices  18.8 us (34%)
  other arithmetic  6.45 us (12%)
  matrix products  5.84 us (11%)
  local copies, waits for them, and re-layouts  2.54 us (5%)
  between operations  0.76 us (1%)
    ppermute x9, waiting for transfers between devices, shift(): return lax.ppermute(x, axis, [(i, (i + k) % n) for i in range(n)])  16.4 us
    ppermute x9, starting transfers between devices, shift(): return lax.ppermute(x, axis, [(i, (i + k) % n) for i in range(n)])  14.9 us
    reduce_sum x1, other arithmetic, kernel_tile(): return jnp.exp(0.1 - jnp.sqrt(jnp.sum(diff * diff, axis=0) + 0.01))  4.65 us
    unnamed x4, matrix products  4.38 us
    all_to_all x1, starting transfers between devices, per_device(): task_blocks = lax.all_to_all(copies, 'task', 0, 0, tiled=True)  3.49 us
    all_to_all x1, waiting for transfers between devices, per_device(): task_blocks = lax.all_to_all(copies, 'task', 0, 0, tiled=True)  2.36 us
    broadcast_in_dim x1, local copies, waits for them, and re-layouts, per_device(): copies = jnp.broadcast_to(task_input[None], (n_task,) + vectors.shape)  1.86 us
    ppermute x2, waiting for transfers between devices, review_the_sums_all(): aux = lax.ppermute(state_now, axis_name=mesh_name, perm=earlier)  1.44 us
  transfers between devices with their start and end apart: 12, of which 6 were waited for; matrix products, arithmetic and copies ran while one was open for 24% of the time, Pallas kernels for 0%

profile of v1, /device:TPU:0, one launch (start us, length us, event | category | flops | bytes accessed | tf_op | source)
XLA Modules:
  0.0 54.5 jit_solution(8346641898152554282)
XLA Ops:
  0.7 3.1 %collective-permute-start = (bf16[3,768]{1,0:T(4,128)(2,1)}, bf16[3,768]{1,0:T(4,128)(2,1)S(1)}, u32[]{:S(2)}, u32[]{:S(2)}) collective-permute-start(bf16[3,768]{1,0:T(4,128)(2,1)} %param.6), channel_id=1, source_target_pairs={{0,4},{4,8},{8,12},{12,0},{1,5},{5,9},{9,13},{13,1},{2,6},{6,10},{... | collective-permute-start | bytes 13832 | tf_op jit(solution)/shard_map/ppermute | solution.py:42
  3.7 2.1 %collective-permute-start.2 = (bf16[3,768]{1,0:T(4,128)(2,1)}, bf16[3,768]{1,0:T(4,128)(2,1)S(1)}, u32[]{:S(2)}, u32[]{:S(2)}) collective-permute-start(bf16[3,768]{1,0:T(4,128)(2,1)} %param.6), channel_id=1, source_target_pairs={{0,12},{4,0},{8,4},{12,8},{1,13},{5,1},{9,5},{13,9},{2,14},{6,2},{... | collective-permute-start | bytes 13832 | tf_op jit(solution)/shard_map/ppermute | solution.py:42
  5.8 3.8 %collective-permute-start.3 = (bf16[2,768,64]{1,2,0:T(8,128)(2,1)}, bf16[2,768,64]{1,2,0:T(8,128)(2,1)S(1)}, u32[]{:S(2)}, u32[]{:S(2)}) collective-permute-start(bf16[2,768,64]{1,2,0:T(8,128)(2,1)} %param.8), channel_id=1, source_target_pairs={{0,12},{4,0},{8,4},{12,8},{1,13},{5,1},{9,5},{13,9},{2,14},{6,2},{... | collective-permute-start | bytes 589832 | tf_op jit(solution)/shard_map/ppermute | solution.py:42
  9.7 0.7 %collective-permute-start.4 = (bf16[3,768]{1,0:T(4,128)(2,1)S(1)}, bf16[3,768]{1,0:T(4,128)(2,1)S(1)}, u32[]{:S(2)}, u32[]{:S(2)}) collective-permute-start(bf16[3,768]{1,0:T(4,128)(2,1)S(1)} %collective-permute-done), channel_id=1, source_target_pairs={{0,4},{4,8},{8,12},{12,0},{1,5},{5,9},{9,13},{13,1},{2,6},{6,10},{... | collective-permute-start | bytes 13832 | tf_op jit(solution)/shard_map/ppermute | solution.py:42
  10.4 0.7 %broadcast_divide_fusion = f32[3]{0:T(128)S(1)} fusion(f32[3]{0:T(128)} %param.7), kind=kLoop, calls=%fused_computation.33 | loop fusion | flops 3 | bytes 24 | tf_op jit(solution)/shard_map/div | solution.py:66
  11.0 11.9 %collective-permute-done.4 = bf16[3,768]{1,0:T(4,128)(2,1)S(1)} collective-permute-done((bf16[3,768]{1,0:T(4,128)(2,1)S(1)}, bf16[3,768]{1,0:T(4,128)(2,1)S(1)}, u32[]{:S(2)}, u32[]{:S(2)}) %collective-permute-start.4) | collective-permute-done | bytes 4640 | tf_op jit(solution)/shard_map/ppermute | solution.py:42
  22.9 1.9 %broadcast_in_dim.4 = bf16[4,2,768,64]{2,3,1,0:T(8,128)(2,1)} broadcast(bf16[2,768,64]{1,2,0:T(8,128)(2,1)} %param.8), dimensions={1,2,3} | broadcast | bytes 983040 | tf_op jit(solution)/shard_map/broadcast_in_dim | solution.py:98
  24.8 3.5 %all-to-all-start = ((bf16[4,2,768,64]{2,3,1,0:T(8,128)(2,1)}), bf16[4,2,768,64]{2,3,1,0:T(8,128)(2,1)S(1)}, u32[]{:S(2)}, u32[]{:S(2)}) async-start(bf16[4,2,768,64]{2,3,1,0:T(8,128)(2,1)} %broadcast_in_dim.4), calls=%async_computation | async-start | bytes 1572864 | tf_op jit(solution)/shard_map/all_to_all | solution.py:99
  28.4 4.7 %multiply_reduce_fusion.2 = (f32[768,768]{1,0:T(8,128)S(1)}, f32[768,768]{1,0:T(8,128)S(1)}, f32[768,768]{1,0:T(8,128)S(1)}, f32[768,768]{1,0:T(8,128)S(1)}) fusion(f32[3,768]{1,0:T(4,128)S(1)} %get-tuple-element.13, f32[3,768]{1,0:T(4,128)S(1)} %get-tuple-element.15, f32[3,768]{1,0:T(4,128)S(1)} %get-tuple-element.14, f32[3,768]{1,0:T(4,128)S(1)} %get-tuple-element.12), kind=kLoop, calls=%fused_computation.2 | loop fusion | flops 18874368 | bytes 9474048 | tf_op jit(solution)/shard_map/reduce_sum | solution.py:38
  33.0 1.1 %fusion = f32[768,128]{0,1:S(1)} fusion(bf16[768,128]{0,1:T(8,128)(2,1)S(1)} %bitcast.48, f32[768,768]{1,0:T(8,128)S(1)} %get-tuple-element.9), kind=kOutput, calls=%fused_computation.10 | convolution fusion | flops 152764416 | bytes 2949120
  34.1 1.1 %fusion.1 = f32[768,128]{0,1:S(1)} fusion(bf16[768,128]{0,1:T(8,128)(2,1)S(1)} %bitcast.57, f32[768,768]{1,0:T(8,128)S(1)} %get-tuple-element.6), kind=kOutput, calls=%fused_computation.11 | convolution fusion | flops 152764416 | bytes 2949120
  35.2 1.1 %fusion.2 = f32[768,128]{0,1:S(1)} fusion(bf16[768,128]{0,1:T(8,128)(2,1)S(1)} %bitcast.56, f32[768,768]{1,0:T(8,128)S(1)} %get-tuple-element.7), kind=kOutput, calls=%fused_computation.12 | convolution fusion | flops 152764416 | bytes 2949120
  36.3 1.1 %fusion.3 = f32[768,128]{0,1:S(1)} fusion(bf16[768,128]{0,1:T(8,128)(2,1)S(1)} %bitcast.55, f32[768,768]{1,0:T(8,128)S(1)} %get-tuple-element.8), kind=kOutput, calls=%fused_computation.13 | convolution fusion | flops 152764416 | bytes 2949120
  37.5 2.4 %all-to-all-done = bf16[4,2,768,64]{2,3,1,0:T(8,128)(2,1)S(1)} async-done(((bf16[4,2,768,64]{2,3,1,0:T(8,128)(2,1)}), bf16[4,2,768,64]{2,3,1,0:T(8,128)(2,1)S(1)}, u32[]{:S(2)}, u32[]{:S(2)}) %all-to-all-start) | async-done | bytes 786464 | tf_op jit(solution)/shard_map/all_to_all | solution.py:99
  39.9 1.4 %collective-permute-done.6 = bf16[1,64,2,768]{3,1,2,0:T(8,128)(2,1)S(1)} collective-permute-done((bf16[1,64,2,768]{3,1,2,0:T(8,128)(2,1)S(1)}, bf16[1,64,2,768]{3,1,2,0:T(8,128)(2,1)S(1)}, u32[]{:S(2)}, u32[]{:S(2)}) %collective-permute-start.6) | collective-permute-done | bytes 196640 | tf_op jit(solution)/shard_map/ppermute | solution.py:20
  41.9 0.5 convolution_bitcast_fusion
  42.6 3.1 %collective-permute-start.10 = (f32[64,256]{1,0:T(8,128)S(1)}, f32[64,256]{1,0:T(8,128)S(1)}, u32[]{:S(2)}, u32[]{:S(2)}) collective-permute-start(f32[64,256]{1,0:T(8,128)S(1)} %reshape.20), channel_id=1, source_target_pairs={{0,8},{4,12},{8,0},{12,4},{1,9},{5,13},{9,1},{13,5},{2,10},{6,14},... | collective-permute-start | bytes 196616 | tf_op jit(solution)/shard_map/ppermute | solution.py:42
  45.7 0.5 collective-permute-start.8
  46.2 1.5 %collective-permute-start.9 = (f32[64,256]{1,0:T(8,128)S(1)}, f32[64,256]{1,0:T(8,128)S(1)}, u32[]{:S(2)}, u32[]{:S(2)}) collective-permute-start(f32[64,256]{1,0:T(8,128)S(1)} %reshape.20), channel_id=1, source_target_pairs={{0,4},{4,8},{8,12},{12,0},{1,5},{5,9},{9,13},{13,1},{2,6},{6,10},{... | collective-permute-start | bytes 196616 | tf_op jit(solution)/shard_map/ppermute | solution.py:42
  47.8 1.8 %collective-permute-done.10 = f32[64,256]{1,0:T(8,128)S(1)} collective-permute-done((f32[64,256]{1,0:T(8,128)S(1)}, f32[64,256]{1,0:T(8,128)S(1)}, u32[]{:S(2)}, u32[]{:S(2)}) %collective-permute-start.10) | collective-permute-done | bytes 65568 | tf_op jit(solution)/shard_map/ppermute | solution.py:42
  49.6 1.3 %collective-permute-done.8 = f32[64,256]{1,0:T(8,128)S(1)} collective-permute-done((f32[64,256]{1,0:T(8,128)S(1)}, f32[64,256]{1,0:T(8,128)S(1)}, u32[]{:S(2)}, u32[]{:S(2)}) %collective-permute-start.8) | collective-permute-done | bytes 65568 | tf_op jit(solution)/shard_map/ppermute | solution.py:42
  50.8 1.4 %collective-permute-done.9 = f32[64,256]{1,0:T(8,128)S(1)} collective-permute-done((f32[64,256]{1,0:T(8,128)S(1)}, f32[64,256]{1,0:T(8,128)S(1)}, u32[]{:S(2)}, u32[]{:S(2)}) %collective-permute-start.9) | collective-permute-done | bytes 65568 | tf_op jit(solution)/shard_map/ppermute | solution.py:42
  52.3 0.6 %add_multiply_fusion = f32[64,256]{1,0:T(8,128)} fusion(f32[64,256]{1,0:T(8,128)S(1)} %collective-permute-done.10, f32[64,256]{1,0:T(8,128)S(1)} %collective-permute-done.9, f32[64,256]{1,0:T(8,128)S(1)} %collective-permute-done.8, f32[64,256]{1,0:T(8,128)S(1)} %reshape.20, pred[]{:T(512)S(6)} %eq.13), kind=kLoop, calls=%fused_computation.26 | loop fusion | flops 98304 | bytes 327681 | tf_op jit(solution)/shard_map/div | solution.py:112
  53.6 0.9 %fusion.4 = bf16[2,768,64]{1,2,0:T(8,128)(2,1)} fusion(bf16[256,2,768]{2,0,1:T(8,128)(2,1)S(1)} %bitcast.45, bf16[2,768,64]{1,2,0:T(8,128)(2,1)S(1)} %copy-done.1, f32[64]{0:T(128)S(1)} %copy-done.3, bf16[256,256]{1,0:T(8,128)(2,1)S(1)} %copy-done, s32[]{:T(128)S(6)} %select_n.42), kind=kOutput, calls=%fused_computation.14 | convolution fusion | flops 50724864 | bytes 1212932 | tf_op jit(solution)/shard_map/asn,ca->snc/dot_general | solution.py:110
  (29 shorter events, 1.6 us)
Async XLA Ops:
  0.6 52.6 %copy-start = (bf16[256,256]{1,0:T(8,128)(2,1)S(1)}, bf16[256,256]{1,0:T(8,128)(2,1)}, u32[]{:S(2)}) copy-start(bf16[256,256]{1,0:T(8,128)(2,1)} %param.9) | copy-start | bytes 393220
  0.6 27.6 %copy-start.2 = (bf16[3,768]{1,0:T(4,128)(2,1)S(1)}, bf16[3,768]{1,0:T(4,128)(2,1)}, u32[]{:S(2)}) copy-start(bf16[3,768]{1,0:T(4,128)(2,1)} %param.6) | copy-start | bytes 13828
  0.7 9.0 %collective-permute-start = (bf16[3,768]{1,0:T(4,128)(2,1)}, bf16[3,768]{1,0:T(4,128)(2,1)S(1)}, u32[]{:S(2)}, u32[]{:S(2)}) collective-permute-start(bf16[3,768]{1,0:T(4,128)(2,1)} %param.6), channel_id=1, source_target_pairs={{0,4},{4,8},{8,12},{12,0},{1,5},{5,9},{9,13},{13,1},{2,6},{6,10},{... | collective-permute-start | bytes 13832 | tf_op jit(solution)/shard_map/ppermute | solution.py:42
  3.7 7.3 %collective-permute-start.2 = (bf16[3,768]{1,0:T(4,128)(2,1)}, bf16[3,768]{1,0:T(4,128)(2,1)S(1)}, u32[]{:S(2)}, u32[]{:S(2)}) collective-permute-start(bf16[3,768]{1,0:T(4,128)(2,1)} %param.6), channel_id=1, source_target_pairs={{0,12},{4,0},{8,4},{12,8},{1,13},{5,1},{9,5},{13,9},{2,14},{6,2},{... | collective-permute-start | bytes 13832 | tf_op jit(solution)/shard_map/ppermute | solution.py:42
  5.8 28.3 %collective-permute-start.1 = (bf16[2,768,64]{1,2,0:T(8,128)(2,1)}, bf16[2,768,64]{1,2,0:T(8,128)(2,1)S(1)}, u32[]{:S(2)}, u32[]{:S(2)}) collective-permute-start(bf16[2,768,64]{1,2,0:T(8,128)(2,1)} %param.8), channel_id=1, source_target_pairs={{0,4},{4,8},{8,12},{12,0},{1,5},{5,9},{9,13},{13,1},{2,6},{6,10},{... | collective-permute-start | bytes 589832 | tf_op jit(solution)/shard_map/ppermute | solution.py:42
  5.8 29.4 %collective-permute-start.3 = (bf16[2,768,64]{1,2,0:T(8,128)(2,1)}, bf16[2,768,64]{1,2,0:T(8,128)(2,1)S(1)}, u32[]{:S(2)}, u32[]{:S(2)}) collective-permute-start(bf16[2,768,64]{1,2,0:T(8,128)(2,1)} %param.8), channel_id=1, source_target_pairs={{0,12},{4,0},{8,4},{12,8},{1,13},{5,1},{9,5},{13,9},{2,14},{6,2},{... | collective-permute-start | bytes 589832 | tf_op jit(solution)/shard_map/ppermute | solution.py:42
  9.6 26.7 %collective-permute-start.5 = (bf16[2,768,64]{1,2,0:T(8,128)(2,1)}, bf16[2,768,64]{1,2,0:T(8,128)(2,1)S(1)}, u32[]{:S(2)}, u32[]{:S(2)}) collective-permute-start(bf16[2,768,64]{1,2,0:T(8,128)(2,1)} %param.8), channel_id=1, source_target_pairs={{0,8},{4,12},{8,0},{12,4},{1,9},{5,13},{9,1},{13,5},{2,10},{6,14},... | collective-permute-start | bytes 589832 | tf_op jit(solution)/shard_map/ppermute | solution.py:42
  9.7 13.2 %collective-permute-start.4 = (bf16[3,768]{1,0:T(4,128)(2,1)S(1)}, bf16[3,768]{1,0:T(4,128)(2,1)S(1)}, u32[]{:S(2)}, u32[]{:S(2)}) collective-permute-start(bf16[3,768]{1,0:T(4,128)(2,1)S(1)} %collective-permute-done), channel_id=1, source_target_pairs={{0,4},{4,8},{8,12},{12,0},{1,5},{5,9},{9,13},{13,1},{2,6},{6,10},{... | collective-permute-start | bytes 13832 | tf_op jit(solution)/shard_map/ppermute | solution.py:42
  24.8 15.1 %all-to-all-start = ((bf16[4,2,768,64]{2,3,1,0:T(8,128)(2,1)}), bf16[4,2,768,64]{2,3,1,0:T(8,128)(2,1)S(1)}, u32[]{:S(2)}, u32[]{:S(2)}) async-start(bf16[4,2,768,64]{2,3,1,0:T(8,128)(2,1)} %broadcast_in_dim.4), calls=%async_computation | async-start | bytes 1572864 | tf_op jit(solution)/shard_map/all_to_all | solution.py:99
  28.4 4.7 %copy-start.1 = (bf16[2,768,64]{1,2,0:T(8,128)(2,1)S(1)}, bf16[2,768,64]{1,2,0:T(8,128)(2,1)}, u32[]{:S(2)}) copy-start(bf16[2,768,64]{1,2,0:T(8,128)(2,1)} %param.8) | copy-start | bytes 589828
  37.4 4.5 %copy-start.4 = (bf16[2]{0:T(256)(128)(2,1)S(1)}, bf16[2]{0:T(256)(128)(2,1)}, u32[]{:S(2)}) copy-start(bf16[2]{0:T(256)(128)(2,1)} %constant.39.clone) | copy-start | bytes 16
  39.9 1.4 %collective-permute-start.6 = (bf16[1,64,2,768]{3,1,2,0:T(8,128)(2,1)S(1)}, bf16[1,64,2,768]{3,1,2,0:T(8,128)(2,1)S(1)}, u32[]{:S(2)}, u32[]{:S(2)}) collective-permute-start(bf16[1,64,2,768]{3,1,2,0:T(8,128)(2,1)S(1)} %bitcast.46), channel_id=1, source_target_pairs={{0,1},{1,0},{2,3},{3,2},{4,5},{5,4},{6,7},{7,6},{8,9},{9,8},{10,11... | collective-permute-start | bytes 589832 | tf_op jit(solution)/shard_map/ppermute | solution.py:20
  41.5 11.5 %collective-permute-start.7 = (bf16[2,64,2,768]{3,1,2,0:T(8,128)(2,1)S(1)}, bf16[2,64,2,768]{3,1,2,0:T(8,128)(2,1)S(1)}, u32[]{:S(2)}, u32[]{:S(2)}) collective-permute-start(bf16[2,64,2,768]{3,1,2,0:T(8,128)(2,1)S(1)} %get-tuple-element.11), channel_id=1, source_target_pairs={{0,2},{1,3},{2,0},{3,1},{4,6},{5,7},{6,4},{7,5},{8,10},{9,11},{10,... | collective-permute-start | bytes 1179656 | tf_op jit(solution)/shard_map/ppermute | solution.py:20
  42.6 6.9 %collective-permute-start.10 = (f32[64,256]{1,0:T(8,128)S(1)}, f32[64,256]{1,0:T(8,128)S(1)}, u32[]{:S(2)}, u32[]{:S(2)}) collective-permute-start(f32[64,256]{1,0:T(8,128)S(1)} %reshape.20), channel_id=1, source_target_pairs={{0,8},{4,12},{8,0},{12,4},{1,9},{5,13},{9,1},{13,5},{2,10},{6,14},... | collective-permute-start | bytes 196616 | tf_op jit(solution)/shard_map/ppermute | solution.py:42
  45.7 5.1 %collective-permute-start.8 = (f32[64,256]{1,0:T(8,128)S(1)}, f32[64,256]{1,0:T(8,128)S(1)}, u32[]{:S(2)}, u32[]{:S(2)}) collective-permute-start(f32[64,256]{1,0:T(8,128)S(1)} %reshape.20), channel_id=1, source_target_pairs={{0,12},{4,0},{8,4},{12,8},{1,13},{5,1},{9,5},{13,9},{2,14},{6,2},{... | collective-permute-start | bytes 196616 | tf_op jit(solution)/shard_map/ppermute | solution.py:42
  46.2 6.1 %collective-permute-start.9 = (f32[64,256]{1,0:T(8,128)S(1)}, f32[64,256]{1,0:T(8,128)S(1)}, u32[]{:S(2)}, u32[]{:S(2)}) collective-permute-start(f32[64,256]{1,0:T(8,128)S(1)} %reshape.20), channel_id=1, source_target_pairs={{0,4},{4,8},{8,12},{12,0},{1,5},{5,9},{9,13},{13,1},{2,6},{6,10},{... | collective-permute-start | bytes 196616 | tf_op jit(solution)/shard_map/ppermute | solution.py:42
  52.9 0.7 %copy-start.3 = (f32[64]{0:T(128)S(1)}, f32[64]{0:T(128)}, u32[]{:S(2)}) copy-start(f32[64]{0:T(128)} %param.10) | copy-start | bytes 772
